TPU v7x, 128 devices: a whole 4x4x4 slice. The times are simulated.
128 devices in a mesh: ctx: 8 (over y, core), head: 16 (over z, x).
Axes of the slice: x: 4, y: 4, z: 4, core: 2. Of those that a mesh axis runs over, the one named last changes fastest.
Arguments:
- conv_input: bfloat16 [32768, 20480], P(('ctx', 'head')), may hold values from -6 to 6
- dt_raw: bfloat16 [32768, 256], P(('ctx', 'head')), as said below
- conv_weight: bfloat16 [4, 20480], replicated, may hold values from -3 to 3
- conv_bias: float32 [20480], replicated, may hold values from -3 to 3
- a_log: float32 [256], replicated, may hold values from -0.2 to 0.2
- dt_bias: float32 [256], replicated, as said below
- d_skip: float32 [256], replicated, may hold values from 0.5 to 1.5
Outputs:
- scan_out: bfloat16 [32768, 16384], P('ctx', 'head')
Inputs may be any that keep to these rules, and one draw needn't show every extreme that they name: softplus(dt_bias[h]) lies between 0.02 / 32768 and 0.04 for every head. softplus(dt_raw[t, h] + dt_bias[h]) lies between 0.02 / 32768 and 0.5 for every token and head.
All inputs are finite; a program needn't handle non-finite values.
Results may differ from a plain program's by a relative error of at most 0.0046.
Values may be sent and summed in bfloat16 or wider, within the bound.
No kernel may reach another device: no remote copies, remote signals or barrier semaphores. Data moves between devices by JAX's collectives and lax.ppermute only.
A program may use at most 256 MiB of HBM per device.

v0:
```python
import jax
import jax.numpy as jnp
from jax import lax
from jax.sharding import PartitionSpec as P

HEADS = 256
HEADDIM = 64
STATE = 256
GROUPS = 8
CONV = 4
SPAN = 512


def shifted(value, axis, by):
    size = lax.axis_size(axis)
    pairs = [(i, i + by) for i in range(size) if 0 <= i + by < size]
    return lax.ppermute(value, axis, pairs)


def prefix(value, axis, combine, identity):
    size, position = (lax.axis_size(axis), lax.axis_index(axis))
    everything = jax.tree.map(lambda part: lax.all_gather(part, axis), value)
    start = jax.tree.map(
        lambda part, zero: jnp.broadcast_to(jnp.asarray(zero, part.dtype), part.shape),
        value,
        identity,
    )

    def turn(k, before):
        reached = k < position
        new = combine(before, jax.tree.map(lambda part: part[k], everything))
        return jax.tree.map(lambda a, b: jnp.where(reached, a, b), new, before)

    return lax.fori_loop(0, size, turn, start)


def compose(earlier, later):
    fade = jnp.exp(jnp.repeat(later[1], HEADDIM, axis=-1))
    return (earlier[0] * fade[..., None, :] + later[0], earlier[1] + later[1])


def on_device(conv_input, dt_raw, conv_weight, conv_bias, a_log, dt_bias, d_skip):
    f32 = jnp.float32
    head_count = lax.axis_size("head")
    heads_dev = HEADS // head_count
    repeat_count = head_count // GROUPS
    head_pos = lax.axis_index("head")
    group = head_pos // repeat_count
    rows = conv_input.shape[0]
    x_width = HEADS * HEADDIM
    slab = heads_dev * HEADDIM
    x_part = conv_input[:, :x_width].reshape(rows, head_count, slab)
    step_part = dt_raw.reshape(rows, head_count, heads_dev)
    arrived, steps = (
        lax.all_to_all(x_part, "head", split_axis=1, concat_axis=0, tiled=True),
        lax.all_to_all(step_part, "head", split_axis=1, concat_axis=0, tiled=True),
    )
    length = arrived.shape[0]
    shared = lax.all_gather(conv_input[:, x_width:], "head", axis=0, tiled=True)
    b_cols = lax.dynamic_slice_in_dim(shared, group * STATE, STATE, 1)
    c_cols = lax.dynamic_slice_in_dim(shared, (GROUPS + group) * STATE, STATE, 1)
    local = jnp.concatenate([arrived.reshape(length, slab), b_cols, c_cols], 1)
    steps = steps.reshape(length, heads_dev)

    def columns(table):
        last = table.ndim - 1
        return jnp.concatenate(
            [
                lax.dynamic_slice_in_dim(table, head_pos * slab, slab, last),
                lax.dynamic_slice_in_dim(table, x_width + group * STATE, STATE, last),
                lax.dynamic_slice_in_dim(table, x_width + (GROUPS + group) * STATE, STATE, last),
            ],
            last,
        )

    kernel = columns(conv_weight).astype(f32)
    offset = columns(conv_bias)
    rim = shifted(local[length - (CONV - 1) :], "ctx", 1)
    padded = jnp.concatenate([rim, local], 0)
    total = padded[0:length].astype(f32) * kernel[0]
    for k in range(1, CONV):
        total = total + padded[k : k + length].astype(f32) * kernel[k]
    act = jax.nn.silu(total + offset).astype(jnp.bfloat16)
    rate = -jnp.exp(lax.dynamic_slice_in_dim(a_log, head_pos * heads_dev, heads_dev, 0))
    bias = lax.dynamic_slice_in_dim(dt_bias, head_pos * heads_dev, heads_dev, 0)
    skip = jnp.repeat(lax.dynamic_slice_in_dim(d_skip, head_pos * heads_dev, heads_dev, 0), HEADDIM)
    step = jax.nn.softplus(steps.astype(f32) + bias)
    blocks = length // SPAN
    x_blocks = act[:, :slab].reshape(blocks, SPAN, slab)
    b_blocks = act[:, slab : slab + STATE].reshape(blocks, SPAN, STATE)
    c_blocks = act[:, slab + STATE :].reshape(blocks, SPAN, STATE)
    step_blocks = step.reshape(blocks, SPAN, heads_dev)
    cum = jnp.cumsum((rate * step).reshape(blocks, SPAN, heads_dev), axis=1)
    tri = lax.broadcasted_iota(jnp.int32, (SPAN, SPAN), 0) >= lax.broadcasted_iota(
        jnp.int32, (SPAN, SPAN), 1
    )

    def local_block(state, inputs):
        x_now, b_now, c_now, step_now, cum_now = inputs
        gram = jnp.dot(c_now, b_now.T, preferred_element_type=f32)
        cum_t = cum_now.T
        decay = jnp.exp(jnp.where(tri[None], cum_t[:, :, None] - cum_t[:, None, :], -jnp.inf))
        mix = (gram[None] * decay * step_now.T[:, None, :]).astype(jnp.bfloat16)
        x_heads = x_now.reshape(SPAN, heads_dev, HEADDIM)
        y_block = jnp.einsum("hts,shp->thp", mix, x_heads, preferred_element_type=f32).reshape(
            SPAN, slab
        )
        weight = jnp.exp(cum_now[-1][None, :] - cum_now) * step_now
        xw = (x_heads.astype(f32) * weight[:, :, None]).astype(jnp.bfloat16).reshape(SPAN, slab)
        contrib = jnp.einsum("sn,sc->nc", b_now, xw, preferred_element_type=f32)
        fade = jnp.exp(jnp.repeat(cum_now[-1], HEADDIM))
        return (state * fade[None, :] + contrib, (y_block, state))

    start_state = jnp.zeros((STATE, slab), f32)
    final, (y_blocks, entering) = lax.scan(
        local_block, start_state, (x_blocks, b_blocks, c_blocks, step_blocks, cum)
    )
    block_totals = cum[:, -1, :]
    totals = jnp.sum(block_totals, axis=0)
    incoming, passed = prefix(
        (final, totals),
        "ctx",
        compose,
        (jnp.zeros((STATE, slab), f32), jnp.zeros((heads_dev,), f32)),
    )
    before = jnp.concatenate(
        [jnp.zeros((1, heads_dev), f32), jnp.cumsum(block_totals, axis=0)[:-1]], 0
    )
    carried = jnp.exp(jnp.repeat(before, HEADDIM, axis=1))[:, None, :] * incoming[None]
    full_state = entering + carried
    grown = jnp.exp(jnp.repeat(cum, HEADDIM, axis=2))
    y_state = grown * jnp.einsum(
        "bqn,bnc->bqc", c_blocks.astype(f32), full_state, precision=lax.Precision.HIGHEST
    )
    result = y_blocks + y_state + skip * x_blocks.astype(f32)
    return result.astype(jnp.bfloat16).reshape(length, slab)


def solution(mesh):
    placed = (P(("ctx", "head"), None), P(("ctx", "head"), None), P(), P(), P(), P(), P())
    return jax.shard_map(
        on_device, mesh=mesh, in_specs=placed, out_specs=P("ctx", "head"), check_vma=False
    )
```

profile of v0, /device:TPU:1, one launch (start us, length us, event | category | flops | bytes accessed | tf_op | source)
XLA Modules:
  0.0 625.6 jit_solution(14649506826397201722)
XLA Ops:
  6.5 3.1 slice.59
  11.4 8.4 %all-to-all-start = ((bf16[256,16,16]{0,2,1:T(8,128)(2,1)}), bf16[256,16,16]{0,2,1:T(8,128)(2,1)S(1)}, u32[]{:S(2)}, u32[]{:S(2)}) async-start(bf16[256,16,16]{0,2,1:T(8,128)(2,1)} %bitcast), calls=%async_computation | async-start | bytes 262144 | tf_op jit(solution)/shard_map/all_to_all | solution.py:56
  19.8 8.5 %slice.58 = bf16[256,16384]{1,0:T(8,128)(2,1)} slice(bf16[256,20480]{1,0:T(8,128)(2,1)} %param.11), slice={[0:256], [0:16384]} | slice | bytes 16777216 | tf_op jit(solution)/shard_map/slice | solution.py:52
  28.2 12.0 %copy.62 = bf16[256,16384]{0,1:T(8,128)(2,1)} copy(bf16[256,16384]{1,0:T(8,128)(2,1)} %slice.58) | data formatting | bytes 16777216
  40.2 12.3 %copy.53 = bf16[256,16,1024]{2,0,1:T(8,128)(2,1)} copy(bf16[256,16,1024]{0,2,1:T(8,128)(2,1)} %bitcast.115) | data formatting | bytes 16777216 | tf_op jit(solution)/shard_map/reshape | solution.py:52
  52.5 6.8 %all-to-all-start.1 = ((bf16[256,16,1024]{2,0,1:T(8,128)(2,1)}), bf16[256,16,1024]{2,0,1:T(8,128)(2,1)}, u32[]{:S(2)}, u32[]{:S(2)}) async-start(bf16[256,16,1024]{2,0,1:T(8,128)(2,1)} %copy.53), calls=%async_computation.1 | async-start | bytes 16777216 | tf_op jit(solution)/shard_map/all_to_all | solution.py:55
  64.0 9.1 %reduce-window.6 = f32[8,16,4,128]{3,1,2,0:T(8,128)S(1)} reduce-window(f32[8,16,4,128]{3,1,2,0:T(8,128)S(1)} %copy.48, f32[]{:T(128)} %constant.84.clone.1), window={size=1x1x1x128 pad=0_0x0_0x0_0x127_0}, to_apply=%region_0.1 | reduce-window | flops 8323072 | bytes 524292 | tf_op jit(solution)/shard_map/reduce-window
  73.6 214.8 %all-gather.5.cloned.1.call-done = bf16[4096,4096]{1,0:T(8,128)(2,1)} async-done(((bf16[256,4096]{1,0:T(8,128)(2,1)}), bf16[4096,4096]{1,0:T(8,128)(2,1)}) %all-gather.5.cloned.1.call-update) | async-done | bytes 33554448 | tf_op jit(solution)/shard_map/all_gather | solution.py:59
  288.5 3.8 constant_dynamic-slice_fusion.6
  292.3 6.0 pad_maximum_fusion
  298.3 3.8 collective-permute-start
  302.9 7.5 %maximum_maximum_fusion = bf16[4099,1536]{1,0:T(8,128)(2,1)S(1)} fusion(bf16[4096,256]{1,0:T(8,128)(2,1)S(1)} %copy-done.2, bf16[4096,256]{1,0:T(8,128)(2,1)S(1)} %get-tuple-element.290, bf16[4096,1024]{1,0:T(8,128)(2,1)} %bitcast.10, bf16[3,1536]{1,0:T(4,128)(2,1)S(1)} %collective-permute-done), kind=kLoop, calls=%fused_computation.32 | loop fusion | flops 50368512 | bytes 25184256 | tf_op jit(solution)/shard_map/concatenate | solution.py:79
  310.4 23.0 %multiply_convert_fusion.3 = bf16[4096,1536]{1,0:T(8,128)(2,1)} fusion(bf16[4099,1536]{1,0:T(8,128)(2,1)S(1)} %maximum_maximum_fusion, f32[1536]{0:T(1024)S(1)} %pad_maximum_fusion.1, f32[1536]{0:T(1024)S(1)} %get-tuple-element.255, f32[1536]{0:T(1024)S(1)} %get-tuple-element.256, f32[1536]{0:T(1024)S(1)} %get-tuple-element.257, ...), kind=kLoop, calls=%fused_computation.30 | loop fusion | flops 138412032 | bytes 62945280 | tf_op jit(solution)/shard_map/convert_element_type | solution.py:83
  333.5 7.8 %slice.85 = bf16[4096,1024]{1,0:T(8,128)(2,1)} slice(bf16[4096,1536]{1,0:T(8,128)(2,1)} %multiply_convert_fusion.3), slice={[0:4096], [0:1024]} | slice | bytes 16777216 | tf_op jit(solution)/shard_map/slice | solution.py:89
  341.2 4.5 fusion.23
  345.7 180.6 %while.29 = (s32[]{:T(128)}, f32[256,1024]{1,0:T(8,128)S(1)}, f32[8,512,1024]{2,1,0:T(8,128)}, f32[8,256,1024]{2,1,0:T(8,128)}, f32[8,512,16]{1,2,0:T(8,128)}, /...) while((s32[]{:T(128)}, f32[256,1024]{1,0:T(8,128)S(1)}, ...), condition=%wide.region_3.4_spmd.clone, body=%wide.region_2.3_spmd.clone.sunk | while | flops 963395584 | bytes 31083584 | solution.py:115
  347.5 2.3 fusion.41
  351.7 7.1 %fusion.42 = f32[16,64,512]{2,1,0:T(8,128)} fusion(bf16[512,16,64]{0,2,1:T(8,128)(2,1)S(1)} %bitcast.110, f32[16,512]{1,0:T(8,128)S(1)} %get-tuple-element.381, f32[16,512]{1,0:T(8,128)S(1)} %get-tuple-element.382, f32[512,512]{1,0:T(8,128)} %fusion.41, pred[512,512]{1,0:T(8,128)(4,1)S(1)} %iota_compare_fusion.2), kind=kOutput, calls=%fused_computation.5.clone.1 | convolution fusion | flops 557842432 | bytes 4521984 | tf_op jit(solution)/shard_map/while/body/eval_jaxpr/hts,shp->thp/dot_general | solution.py:105
  358.8 1.9 copy.81
  370.0 2.3 fusion.41
  374.3 7.1 %fusion.42 = f32[16,64,512]{2,1,0:T(8,128)} fusion(bf16[512,16,64]{0,2,1:T(8,128)(2,1)S(1)} %bitcast.110, f32[16,512]{1,0:T(8,128)S(1)} %get-tuple-element.381, f32[16,512]{1,0:T(8,128)S(1)} %get-tuple-element.382, f32[512,512]{1,0:T(8,128)} %fusion.41, pred[512,512]{1,0:T(8,128)(4,1)S(1)} %iota_compare_fusion.2), kind=kOutput, calls=%fused_computation.5.clone.1 | convolution fusion | flops 557842432 | bytes 4521984 | tf_op jit(solution)/shard_map/while/body/eval_jaxpr/hts,shp->thp/dot_general | solution.py:105
  381.4 1.9 copy.81
  392.7 2.3 fusion.41
  396.9 7.1 %fusion.42 = f32[16,64,512]{2,1,0:T(8,128)} fusion(bf16[512,16,64]{0,2,1:T(8,128)(2,1)S(1)} %bitcast.110, f32[16,512]{1,0:T(8,128)S(1)} %get-tuple-element.381, f32[16,512]{1,0:T(8,128)S(1)} %get-tuple-element.382, f32[512,512]{1,0:T(8,128)} %fusion.41, pred[512,512]{1,0:T(8,128)(4,1)S(1)} %iota_compare_fusion.2), kind=kOutput, calls=%fused_computation.5.clone.1 | convolution fusion | flops 557842432 | bytes 4521984 | tf_op jit(solution)/shard_map/while/body/eval_jaxpr/hts,shp->thp/dot_general | solution.py:105
  415.2 2.3 fusion.41
  419.5 7.1 %fusion.42 = f32[16,64,512]{2,1,0:T(8,128)} fusion(bf16[512,16,64]{0,2,1:T(8,128)(2,1)S(1)} %bitcast.110, f32[16,512]{1,0:T(8,128)S(1)} %get-tuple-element.381, f32[16,512]{1,0:T(8,128)S(1)} %get-tuple-element.382, f32[512,512]{1,0:T(8,128)} %fusion.41, pred[512,512]{1,0:T(8,128)(4,1)S(1)} %iota_compare_fusion.2), kind=kOutput, calls=%fused_computation.5.clone.1 | convolution fusion | flops 557842432 | bytes 4521984 | tf_op jit(solution)/shard_map/while/body/eval_jaxpr/hts,shp->thp/dot_general | solution.py:105
  437.7 2.3 fusion.41
  442.0 7.1 %fusion.42 = f32[16,64,512]{2,1,0:T(8,128)} fusion(bf16[512,16,64]{0,2,1:T(8,128)(2,1)S(1)} %bitcast.110, f32[16,512]{1,0:T(8,128)S(1)} %get-tuple-element.381, f32[16,512]{1,0:T(8,128)S(1)} %get-tuple-element.382, f32[512,512]{1,0:T(8,128)} %fusion.41, pred[512,512]{1,0:T(8,128)(4,1)S(1)} %iota_compare_fusion.2), kind=kOutput, calls=%fused_computation.5.clone.1 | convolution fusion | flops 557842432 | bytes 4521984 | tf_op jit(solution)/shard_map/while/body/eval_jaxpr/hts,shp->thp/dot_general | solution.py:105
  460.3 2.3 fusion.41
  464.6 7.1 %fusion.42 = f32[16,64,512]{2,1,0:T(8,128)} fusion(bf16[512,16,64]{0,2,1:T(8,128)(2,1)S(1)} %bitcast.110, f32[16,512]{1,0:T(8,128)S(1)} %get-tuple-element.381, f32[16,512]{1,0:T(8,128)S(1)} %get-tuple-element.382, f32[512,512]{1,0:T(8,128)} %fusion.41, pred[512,512]{1,0:T(8,128)(4,1)S(1)} %iota_compare_fusion.2), kind=kOutput, calls=%fused_computation.5.clone.1 | convolution fusion | flops 557842432 | bytes 4521984 | tf_op jit(solution)/shard_map/while/body/eval_jaxpr/hts,shp->thp/dot_general | solution.py:105
  482.9 2.3 fusion.41
  487.1 7.1 %fusion.42 = f32[16,64,512]{2,1,0:T(8,128)} fusion(bf16[512,16,64]{0,2,1:T(8,128)(2,1)S(1)} %bitcast.110, f32[16,512]{1,0:T(8,128)S(1)} %get-tuple-element.381, f32[16,512]{1,0:T(8,128)S(1)} %get-tuple-element.382, f32[512,512]{1,0:T(8,128)} %fusion.41, pred[512,512]{1,0:T(8,128)(4,1)S(1)} %iota_compare_fusion.2), kind=kOutput, calls=%fused_computation.5.clone.1 | convolution fusion | flops 557842432 | bytes 4521984 | tf_op jit(solution)/shard_map/while/body/eval_jaxpr/hts,shp->thp/dot_general | solution.py:105
  505.5 2.3 fusion.41
  509.8 7.1 %fusion.42 = f32[16,64,512]{2,1,0:T(8,128)} fusion(bf16[512,16,64]{0,2,1:T(8,128)(2,1)S(1)} %bitcast.110, f32[16,512]{1,0:T(8,128)S(1)} %get-tuple-element.381, f32[16,512]{1,0:T(8,128)S(1)} %get-tuple-element.382, f32[512,512]{1,0:T(8,128)} %fusion.41, pred[512,512]{1,0:T(8,128)(4,1)S(1)} %iota_compare_fusion.2), kind=kOutput, calls=%fused_computation.5.clone.1 | convolution fusion | flops 557842432 | bytes 4521984 | tf_op jit(solution)/shard_map/while/body/eval_jaxpr/hts,shp->thp/dot_general | solution.py:105
  530.3 13.1 %all-reduce.1 = f32[128]{0:T(128)S(1)} all-reduce(f32[128]{0:T(128)S(1)} %dynamic-update-slice), channel_id=2, replica_groups=mesh['ctx'=8,'head'=16] {'ctx'}, use_global_device_ids=true, to_apply=%add.1 | all-reduce | flops 128 | bytes 1024
  543.8 8.1 %broadcast_in_dim.62 = f32[8,512,16,64]{1,3,2,0:T(8,128)} broadcast(f32[8,512,16]{1,2,0:T(8,128)S(1)} %fusion.22), dimensions={0,1,2} | broadcast | bytes 17039360 | tf_op jit(solution)/shard_map/broadcast_in_dim | solution.py:131
  551.9 16.7 %copy.56 = f32[8,512,1024]{2,1,0:T(8,128)} copy(f32[8,512,1024]{1,2,0:T(8,128)} %bitcast.112) | data formatting | bytes 33554432 | tf_op jit(solution)/shard_map/exp | solution.py:131
  568.6 9.4 %all-gather.7.cloned.1.call-done = f32[2048,1024]{1,0:T(8,128)} async-done(((f32[256,1024]{1,0:T(8,128)}), f32[2048,1024]{1,0:T(8,128)}) %all-gather.7.cloned.1.call-update) | async-done | bytes 8388624 | tf_op jit(solution)/shard_map/all_gather | solution.py:22
  578.0 18.5 %while.30 = (s32[]{:T(128)}, f32[256,1024]{1,0:T(8,128)S(1)}, s32[]{:T(128)}, f32[8,16]{1,0:T(8,128)S(1)}, f32[8,256,1024]{2,1,0:T(8,128)}, /*index=5*/s32[]{:T(128)}, s32[]{:T(128)}) while((s32[]{:T(128)}, f32[256,1024]{1,0:T(8,128)S(1)}, s32[]{:T(128)}, f32[8,16]{1,0:T(8,128)S(1)}, f32[8,256,1024]{2,1,0:T(8,128)}, ...), condition=%wide.region_7.8_spmd.clone, body=%wide.region_6.7_spmd.clone.sunk | while | flops 1048580 | bytes 3162409 | solution.py:34
  578.2 2.1 fusion.43
  580.5 2.1 fusion.43
  582.8 2.1 fusion.43
  585.1 2.1 fusion.43
  587.4 2.1 fusion.43
  589.7 2.1 fusion.43
  592.1 2.1 fusion.43
  594.4 2.1 fusion.43
  596.5 22.2 %add_convert_fusion = bf16[8,512,1024]{2,1,0:T(8,128)(2,1)} fusion(bf16[8,512,1024]{2,1,0:T(8,128)(2,1)} %get-tuple-element.449, f32[8,512,1024]{2,1,0:T(8,128)} %get-tuple-element.153, f32[8,512,1024]{2,1,0:T(8,128)} %copy.56, bf16[8,512,256]{2,1,0:T(8,128)(2,1)} %bitcast.13, f32[1024]{0:T(1024)S(1)} %mul.190, f32[8,256,1024]{2,1,0:T(8,128)} %get-tuple-element.154, ...), kind=kOutput, calls=%fused_computation.31 | convolution fusion | flops 12914262016 | bytes 61902848 | tf_op jit(solution)/shard_map/bqn,bnc->bqc/dot_general | solution.py:132
  (216 shorter events, 113.1 us)
Async XLA Ops:
  6.5 281.9 %all-gather.5.cloned.1.call-start = ((), (), s32[]{:S(2)}) async-start(), calls=%async_computation.2 | async-start | bytes 35651584 | tf_op jit(solution)/shard_map/all_gather | solution.py:59
  11.4 41.2 %all-to-all-start = ((bf16[256,16,16]{0,2,1:T(8,128)(2,1)}), bf16[256,16,16]{0,2,1:T(8,128)(2,1)S(1)}, u32[]{:S(2)}, u32[]{:S(2)}) async-start(bf16[256,16,16]{0,2,1:T(8,128)(2,1)} %bitcast), calls=%async_computation | async-start | bytes 262144 | tf_op jit(solution)/shard_map/all_to_all | solution.py:56
  52.5 7.7 %copy-start.3 = (f32[256]{0:T(256)S(1)}, f32[256]{0:T(256)}, u32[]{:S(2)}) copy-start(f32[256]{0:T(256)} %param.16) | copy-start | bytes 3076
  52.5 7.8 %copy-start.4 = (f32[256]{0:T(256)S(1)}, f32[256]{0:T(256)}, u32[]{:S(2)}) copy-start(f32[256]{0:T(256)} %param.15) | copy-start | bytes 3076
  52.5 239.8 %all-to-all-start.1 = ((bf16[256,16,1024]{2,0,1:T(8,128)(2,1)}), bf16[256,16,1024]{2,0,1:T(8,128)(2,1)}, u32[]{:S(2)}, u32[]{:S(2)}) async-start(bf16[256,16,1024]{2,0,1:T(8,128)(2,1)} %copy.53), calls=%async_computation.1 | async-start | bytes 16777216 | tf_op jit(solution)/shard_map/all_to_all | solution.py:55
  59.4 518.6 %all-gather.7.cloned.1.call-start = ((), (), s32[]{:S(2)}) async-start(), calls=%async_computation.3 | async-start | bytes 9437184 | tf_op jit(solution)/shard_map/all_gather | solution.py:22
  292.3 10.7 %copy-start.2 = (bf16[4096,256]{1,0:T(8,128)(2,1)S(1)}, bf16[4096,256]{1,0:T(8,128)(2,1)}, u32[]{:S(2)}) copy-start(bf16[4096,256]{1,0:T(8,128)(2,1)} %get-tuple-element.291) | copy-start | bytes 6291460
  298.3 4.6 collective-permute-start
  345.7 181.7 %copy-start.5 = (f32[256]{0:T(256)S(1)}, f32[256]{0:T(256)}, u32[]{:S(2)}) copy-start(f32[256]{0:T(256)} %param.17) | copy-start | bytes 3076
  345.7 181.9 %copy-start.6 = (u32[128]{0:T(128)S(1)}, u32[128]{0:T(128)}, u32[]{:S(2)}) copy-start(u32[128]{0:T(128)} %constant.103) | copy-start | bytes 1540
  351.6 7.2 %copy-start.1 = (bf16[1,512,1024]{1,2,0:T(8,128)(2,1)}, bf16[1,512,1024]{1,2,0:T(8,128)(2,1)S(1)}, u32[]{:S(2)}) copy-start(bf16[1,512,1024]{1,2,0:T(8,128)(2,1)S(1)} %copy.80) | copy-start | bytes 3145732 | tf_op jit(solution)/shard_map/while
  374.2 7.2 %copy-start.1 = (bf16[1,512,1024]{1,2,0:T(8,128)(2,1)}, bf16[1,512,1024]{1,2,0:T(8,128)(2,1)S(1)}, u32[]{:S(2)}) copy-start(bf16[1,512,1024]{1,2,0:T(8,128)(2,1)S(1)} %copy.80) | copy-start | bytes 3145732 | tf_op jit(solution)/shard_map/while
  396.8 7.2 %copy-start.1 = (bf16[1,512,1024]{1,2,0:T(8,128)(2,1)}, bf16[1,512,1024]{1,2,0:T(8,128)(2,1)S(1)}, u32[]{:S(2)}) copy-start(bf16[1,512,1024]{1,2,0:T(8,128)(2,1)S(1)} %copy.80) | copy-start | bytes 3145732 | tf_op jit(solution)/shard_map/while
  419.4 7.2 %copy-start.1 = (bf16[1,512,1024]{1,2,0:T(8,128)(2,1)}, bf16[1,512,1024]{1,2,0:T(8,128)(2,1)S(1)}, u32[]{:S(2)}) copy-start(bf16[1,512,1024]{1,2,0:T(8,128)(2,1)S(1)} %copy.80) | copy-start | bytes 3145732 | tf_op jit(solution)/shard_map/while
  441.9 7.2 %copy-start.1 = (bf16[1,512,1024]{1,2,0:T(8,128)(2,1)}, bf16[1,512,1024]{1,2,0:T(8,128)(2,1)S(1)}, u32[]{:S(2)}) copy-start(bf16[1,512,1024]{1,2,0:T(8,128)(2,1)S(1)} %copy.80) | copy-start | bytes 3145732 | tf_op jit(solution)/shard_map/while
  464.5 7.2 %copy-start.1 = (bf16[1,512,1024]{1,2,0:T(8,128)(2,1)}, bf16[1,512,1024]{1,2,0:T(8,128)(2,1)S(1)}, u32[]{:S(2)}) copy-start(bf16[1,512,1024]{1,2,0:T(8,128)(2,1)S(1)} %copy.80) | copy-start | bytes 3145732 | tf_op jit(solution)/shard_map/while
  487.1 7.2 %copy-start.1 = (bf16[1,512,1024]{1,2,0:T(8,128)(2,1)}, bf16[1,512,1024]{1,2,0:T(8,128)(2,1)S(1)}, u32[]{:S(2)}) copy-start(bf16[1,512,1024]{1,2,0:T(8,128)(2,1)S(1)} %copy.80) | copy-start | bytes 3145732 | tf_op jit(solution)/shard_map/while
  509.7 7.2 %copy-start.1 = (bf16[1,512,1024]{1,2,0:T(8,128)(2,1)}, bf16[1,512,1024]{1,2,0:T(8,128)(2,1)S(1)}, u32[]{:S(2)}) copy-start(bf16[1,512,1024]{1,2,0:T(8,128)(2,1)S(1)} %copy.80) | copy-start | bytes 3145732 | tf_op jit(solution)/shard_map/while
  526.3 1.0 copy-start
Sparse Core Ops, SparseCore 0:
  9.8 278.5 all-gather.4
  527.5 50.5 all-gather.6
where the time goes:
time: 631 us; the launch traced here: 626 us
  waiting for transfers between devices  224 us (35%)
  local copies, waits for them, and re-layouts  150 us (24%)
  matrix products  111 us (18%)
  other arithmetic  93.5 us (15%)
  starting transfers between devices  19.1 us (3%)
  between operations  14.4 us (2%)
  blocking collectives  13.1 us (2%)
    all_gather x1, waiting for transfers between devices, on_device(): shared = lax.all_gather(conv_input[:, x_width:], 'head', axis=0, tiled=True)  215 us
    dot_general x8, matrix products, local_block(): jnp.einsum('hts,shp->thp', mix, x_heads, preferred_element_type=f32)  57 us
    dynamic_update_slice x16, local copies, waits for them, and re-layouts, on_device(): lax.scan(local_block, start_state, (x_blocks, b_blocks, c_blocks, step_bl...  27.1 us
    convert_element_type x1, other arithmetic, on_device(): act = jax.nn.silu(total + offset).astype(jnp.bfloat16)  23 us
    dynamic_slice x24, local copies, waits for them, and re-layouts, on_device(): lax.scan(local_block, start_state, (x_blocks, b_blocks, c_blocks, step_bl...  22.6 us
    dot_general x1, matrix products, on_device(): jnp.einsum('bqn,bnc->bqc', c_blocks.astype(f32), full_state, precision=la...  22.2 us
    dot_general x8, matrix products, local_block(): gram = jnp.dot(c_now, b_now.T, preferred_element_type=f32)  18.5 us
    select_n x8, other arithmetic, turn(): return jax.tree.map(lambda a, b: jnp.where(reached, a, b), new, before)  17.1 us
  transfers between devices with their start and end apart: 5, of which 2 were waited for; matrix products, arithmetic and copies ran while one was open for 13% of the time, Pallas kernels for 0%

commit v1 on v0

--- a/solution.py
+++ b/solution.py
@@ -56,7 +56,10 @@
         lax.all_to_all(step_part, "head", split_axis=1, concat_axis=0, tiled=True),
     )
     length = arrived.shape[0]
-    shared = lax.all_gather(conv_input[:, x_width:], "head", axis=0, tiled=True)
+    shared = jnp.concatenate(
+        lax.all_to_all(jnp.stack([conv_input[:, x_width:]] * lax.axis_size("head")), "head", 0, 0),
+        axis=0,
+    )
     b_cols = lax.dynamic_slice_in_dim(shared, group * STATE, STATE, 1)
     c_cols = lax.dynamic_slice_in_dim(shared, (GROUPS + group) * STATE, STATE, 1)
     local = jnp.concatenate([arrived.reshape(length, slab), b_cols, c_cols], 1)

time: 631 us -> 1000 us (1.58)
  waiting for transfers between devices: 224 us -> 579 us
    all_to_all x0 -> x1, waiting for transfers between devices: none -> 463 us  [on_device(): lax.all_to_all(jnp.stack([conv_input[:, x_width:]] * lax.axis_size('head'...]
    all_gather x1 -> x0, waiting for transfers between devices: 215 us -> none  [on_device(): shared = lax.all_gather(conv_input[:, x_width:], 'head', axis=0, tiled=True)]
    all_to_all x1, waiting for transfers between devices: 0.01 us -> 101 us  [on_device(): lax.all_to_all(x_part, 'head', split_axis=1, concat_axis=0, tiled=True)]
    another operation x3 -> x4, local copies, waits for them, and re-layouts: 0.17 us -> 11.1 us  [the longest x1 10.9 us: on_device(): jnp.stack([conv_input[:, x_width:]] * lax.axis_size('head'))]
  transfers between devices with their start and end apart: 5 -> 5, of which waited for: 2 -> 4; matrix products, arithmetic and copies ran while one was open for 13% -> 8% of each run, Pallas kernels for 0% -> 0%
where the time goes in v1:
time: 1000 us; the launch traced here: 995 us
  waiting for transfers between devices  579 us (58%)
  local copies, waits for them, and re-layouts  158 us (16%)
  matrix products  111 us (11%)
  other arithmetic  93.5 us (9%)
  starting transfers between devices  26.1 us (3%)
  between operations  14.4 us (1%)
  blocking collectives  13 us (1%)
    all_to_all x1, waiting for transfers between devices, on_device(): lax.all_to_all(jnp.stack([conv_input[:, x_width:]] * lax.axis_size('head'...  463 us
    all_to_all x1, waiting for transfers between devices, on_device(): lax.all_to_all(x_part, 'head', split_axis=1, concat_axis=0, tiled=True)  101 us
    dot_general x8, matrix products, local_block(): jnp.einsum('hts,shp->thp', mix, x_heads, preferred_element_type=f32)  57 us
    dynamic_update_slice x16, local copies, waits for them, and re-layouts, on_device(): lax.scan(local_block, start_state, (x_blocks, b_blocks, c_blocks, step_bl...  27.1 us
    convert_element_type x1, other arithmetic, on_device(): act = jax.nn.silu(total + offset).astype(jnp.bfloat16)  23 us
    dynamic_slice x24, local copies, waits for them, and re-layouts, on_device(): lax.scan(local_block, start_state, (x_blocks, b_blocks, c_blocks, step_bl...  22.6 us
    dot_general x1, matrix products, on_device(): jnp.einsum('bqn,bnc->bqc', c_blocks.astype(f32), full_state, precision=la...  22.2 us
  transfers between devices with their start and end apart: 5, of which 4 were waited for; matrix products, arithmetic and copies ran while one was open for 8% of the time, Pallas kernels for 0%

profile of v1, /device:TPU:1, one launch (start us, length us, event | category | flops | bytes accessed | tf_op | source)
XLA Modules:
  0.0 995.4 jit_solution(10374806808446951511)
XLA Ops:
  8.2 8.4 all-to-all-start
  18.4 5.1 all-to-all-done
  23.5 10.9 %stack.2 = bf16[16,256,4096]{2,1,0:T(8,128)(2,1)} broadcast(bf16[256,4096]{1,0:T(8,128)(2,1)S(1)} %slice.59), dimensions={1,2} | broadcast | bytes 35651584 | tf_op jit(solution)/shard_map/stack | solution.py:60
  34.4 6.0 all-to-all-start.2
  40.4 7.7 slice.58
  48.0 11.9 %copy.62 = bf16[256,16384]{0,1:T(8,128)(2,1)} copy(bf16[256,16384]{1,0:T(8,128)(2,1)} %slice.58) | data formatting | bytes 16777216
  59.9 12.2 %copy.53 = bf16[256,16,1024]{2,0,1:T(8,128)(2,1)} copy(bf16[256,16,1024]{0,2,1:T(8,128)(2,1)} %bitcast.116) | data formatting | bytes 16777216 | tf_op jit(solution)/shard_map/reshape | solution.py:52
  72.2 463.3 %all-to-all-done.2 = bf16[16,256,4096]{2,1,0:T(8,128)(2,1)} async-done(((bf16[16,256,4096]{2,1,0:T(8,128)(2,1)}), bf16[16,256,4096]{2,1,0:T(8,128)(2,1)}, u32[]{:S(2)}, u32[]{:S(2)}) %all-to-all-start.2) | async-done | bytes 33554464 | tf_op jit(solution)/shard_map/all_to_all | solution.py:60
  535.4 4.7 all-to-all-start.1
  544.8 9.1 reduce-window.6
  554.4 3.8 constant_dynamic-slice_fusion.6
  558.3 101.4 %all-to-all-done.1 = bf16[256,16,1024]{2,0,1:T(8,128)(2,1)} async-done(((bf16[256,16,1024]{2,0,1:T(8,128)(2,1)}), bf16[256,16,1024]{2,0,1:T(8,128)(2,1)}, u32[]{:S(2)}, u32[]{:S(2)}) %all-to-all-start.1) | async-done | bytes 8388640 | tf_op jit(solution)/shard_map/all_to_all | solution.py:55
  659.7 6.0 pad_maximum_fusion
  665.7 7.0 collective-permute-start
  673.5 7.5 maximum_maximum_fusion
  681.0 23.0 %multiply_convert_fusion.3 = bf16[4096,1536]{1,0:T(8,128)(2,1)} fusion(bf16[4099,1536]{1,0:T(8,128)(2,1)S(1)} %maximum_maximum_fusion, f32[1536]{0:T(1024)S(1)} %pad_maximum_fusion.1, f32[1536]{0:T(1024)S(1)} %get-tuple-element.255, f32[1536]{0:T(1024)S(1)} %get-tuple-element.256, f32[1536]{0:T(1024)S(1)} %get-tuple-element.257, ...), kind=kLoop, calls=%fused_computation.30 | loop fusion | flops 138412032 | bytes 62945280 | tf_op jit(solution)/shard_map/convert_element_type | solution.py:86
  704.0 7.8 slice.85
  711.8 4.5 fusion.23
  716.2 180.6 %while.29 = (s32[]{:T(128)}, f32[256,1024]{1,0:T(8,128)S(1)}, f32[8,512,1024]{2,1,0:T(8,128)}, f32[8,256,1024]{2,1,0:T(8,128)}, f32[8,512,16]{1,2,0:T(8,128)}, /...) while((s32[]{:T(128)}, f32[256,1024]{1,0:T(8,128)S(1)}, ...), condition=%wide.region_3.4_spmd.clone, body=%wide.region_2.3_spmd.clone.sunk | while | flops 963395584 | bytes 31083584 | solution.py:118
  718.0 2.3 fusion.41
  722.3 7.1 fusion.42
  740.6 2.3 fusion.41
  744.8 7.1 fusion.42
  763.2 2.3 fusion.41
  767.5 7.1 fusion.42
  785.8 2.3 fusion.41
  790.0 7.1 fusion.42
  808.3 2.3 fusion.41
  812.6 7.1 fusion.42
  830.9 2.3 fusion.41
  835.1 7.1 fusion.42
  853.5 2.3 fusion.41
  857.7 7.1 fusion.42
  876.1 2.3 fusion.41
  880.3 7.1 fusion.42
  900.9 13.0 %all-reduce.1 = f32[128]{0:T(128)S(1)} all-reduce(f32[128]{0:T(128)S(1)} %dynamic-update-slice), channel_id=2, replica_groups=mesh['ctx'=8,'head'=16] {'ctx'}, use_global_device_ids=true, to_apply=%add.1 | all-reduce | flops 128 | bytes 1024
  914.4 8.1 broadcast_in_dim.62
  922.4 16.5 %copy.56 = f32[8,512,1024]{2,1,0:T(8,128)} copy(f32[8,512,1024]{1,2,0:T(8,128)} %bitcast.113) | data formatting | bytes 33554432 | tf_op jit(solution)/shard_map/exp | solution.py:134
  938.9 8.9 all-gather.4.cloned.1.call-done
  947.8 18.5 %while.30 = (s32[]{:T(128)}, f32[256,1024]{1,0:T(8,128)S(1)}, s32[]{:T(128)}, f32[8,16]{1,0:T(8,128)S(1)}, f32[8,256,1024]{2,1,0:T(8,128)}, /*index=5*/s32[]{:T(128)}, s32[]{:T(128)}) while((s32[]{:T(128)}, f32[256,1024]{1,0:T(8,128)S(1)}, s32[]{:T(128)}, f32[8,16]{1,0:T(8,128)S(1)}, f32[8,256,1024]{2,1,0:T(8,128)}, ...), condition=%wide.region_7.8_spmd.clone, body=%wide.region_6.7_spmd.clone.sunk | while | flops 1048580 | bytes 3162409 | solution.py:34
  947.9 2.1 fusion.43
  950.3 2.1 fusion.43
  952.6 2.1 fusion.43
  954.9 2.1 fusion.43
  957.2 2.1 fusion.43
  959.5 2.1 fusion.43
  961.8 2.1 fusion.43
  966.3 22.2 %add_convert_fusion = bf16[8,512,1024]{2,1,0:T(8,128)(2,1)} fusion(bf16[8,512,1024]{2,1,0:T(8,128)(2,1)} %get-tuple-element.450, f32[8,512,1024]{2,1,0:T(8,128)} %get-tuple-element.153, f32[8,512,1024]{2,1,0:T(8,128)} %copy.56, bf16[8,512,256]{2,1,0:T(8,128)(2,1)} %bitcast.14, f32[1024]{0:T(1024)S(1)} %mul.190, f32[8,256,1024]{2,1,0:T(8,128)} %get-tuple-element.154, ...), kind=kOutput, calls=%fused_computation.31 | convolution fusion | flops 12914262016 | bytes 61902848 | tf_op jit(solution)/shard_map/bqn,bnc->bqc/dot_general | solution.py:135
  (216 shorter events, 120.8 us)
Async XLA Ops:
  8.2 15.3 %all-to-all-start = ((bf16[256,16,16]{0,2,1:T(8,128)(2,1)}), bf16[256,16,16]{0,2,1:T(8,128)(2,1)S(1)}, u32[]{:S(2)}, u32[]{:S(2)}) async-start(bf16[256,16,16]{0,2,1:T(8,128)(2,1)} %bitcast), calls=%async_computation | async-start | bytes 262144 | tf_op jit(solution)/shard_map/all_to_all | solution.py:56
  34.4 501.0 %all-to-all-start.2 = ((bf16[16,256,4096]{2,1,0:T(8,128)(2,1)}), bf16[16,256,4096]{2,1,0:T(8,128)(2,1)}, u32[]{:S(2)}, u32[]{:S(2)}) async-start(bf16[16,256,4096]{2,1,0:T(8,128)(2,1)} %stack.2), calls=%async_computation.2 | async-start | bytes 67108864 | tf_op jit(solution)/shard_map/all_to_all | solution.py:60
  72.2 468.8 %copy-start.3 = (f32[256]{0:T(256)S(1)}, f32[256]{0:T(256)}, u32[]{:S(2)}) copy-start(f32[256]{0:T(256)} %param.16) | copy-start | bytes 3076
  72.2 468.9 %copy-start.4 = (f32[256]{0:T(256)S(1)}, f32[256]{0:T(256)}, u32[]{:S(2)}) copy-start(f32[256]{0:T(256)} %param.15) | copy-start | bytes 3076
  535.4 124.2 %all-to-all-start.1 = ((bf16[256,16,1024]{2,0,1:T(8,128)(2,1)}), bf16[256,16,1024]{2,0,1:T(8,128)(2,1)}, u32[]{:S(2)}, u32[]{:S(2)}) async-start(bf16[256,16,1024]{2,0,1:T(8,128)(2,1)} %copy.53), calls=%async_computation.1 | async-start | bytes 16777216 | tf_op jit(solution)/shard_map/all_to_all | solution.py:55
  540.2 407.6 %all-gather.4.cloned.1.call-start = ((), (), s32[]{:S(2)}) async-start(), calls=%async_computation.3 | async-start | bytes 9437184 | tf_op jit(solution)/shard_map/all_gather | solution.py:22
  659.7 13.8 %copy-start.2 = (bf16[4096,256]{1,0:T(8,128)(2,1)S(1)}, bf16[4096,256]{1,0:T(8,128)(2,1)}, u32[]{:S(2)}) copy-start(bf16[4096,256]{1,0:T(8,128)(2,1)} %get-tuple-element.291) | copy-start | bytes 6291460
  665.7 7.8 collective-permute-start
  716.2 181.7 %copy-start.5 = (f32[256]{0:T(256)S(1)}, f32[256]{0:T(256)}, u32[]{:S(2)}) copy-start(f32[256]{0:T(256)} %param.17) | copy-start | bytes 3076
  716.2 181.9 %copy-start.6 = (u32[128]{0:T(128)S(1)}, u32[128]{0:T(128)}, u32[]{:S(2)}) copy-start(u32[128]{0:T(128)} %constant.103) | copy-start | bytes 1540
  722.2 7.2 copy-start.1
  744.7 7.2 copy-start.1
  767.4 7.2 copy-start.1
  789.9 7.2 copy-start.1
  812.5 7.2 copy-start.1
  835.0 7.2 copy-start.1
  857.6 7.2 copy-start.1
  880.2 7.2 copy-start.1
  896.9 1.0 copy-start
Sparse Core Ops, SparseCore 0:
  898.0 49.7 all-gather.3
